TPU v7x, 32 devices: a whole 2x2x4 slice. The times are simulated.
32 devices in a mesh: mem: 4 (over z), tile: 8 (over y, x, core).
Axes of the slice: x: 2, y: 2, z: 4, core: 2. Of those that a mesh axis runs over, the one named last changes fastest.
Arguments:
- source_blocks: bfloat16 [1024, 8, 2, 256], P('tile', 'mem'), may hold values from -6 to 6
- send_blocks: int32 [8, 8, 24], P('tile'), may hold values from 0 to 127
- recv_slot: int32 [8, 8, 24], P('tile'), may hold values from 0 to 95
- recv_weight: float32 [8, 8, 24], P('tile'), may hold values from 0.25 to 2
- recv_count: int32 [8, 8], P('tile'), may hold values from 0 to 24, as said below
- regional: bfloat16 [8, 2, 512, 384], P('mem', None, 'tile'), may hold values from -6 to 6
- x_operator: bfloat16 [512, 512], P(('mem', 'tile'))
- y_operator: bfloat16 [384, 384], P(('mem', 'tile'))
Outputs:
- blended: bfloat16 [8, 2, 512, 384], P('mem', None, 'tile')
Inputs may be any that keep to these rules, and one draw needn't show every extreme that they name: `recv_count`: live entries of one pair of tiles number at most 24; some pairs in every draw have 24.
All inputs are finite; a program needn't handle non-finite values.
Results may differ from a plain program's by a relative error of at most 0.0055.
Values may be sent and summed in bfloat16 or wider, within the bound.
No kernel may reach another device: no remote copies, remote signals or barrier semaphores. Data moves between devices by JAX's collectives and lax.ppermute only.
A program may use at most 128 MiB of HBM per device.

v0:
```python
import math
import jax
import jax.numpy as jnp
from jax import lax
from jax.sharding import PartitionSpec as P


def xor_gather(data, axis_name, groups):
    count = lax.axis_size(axis_name)
    for group in groups:
        parts = [data]
        for code in range(1, 1 << len(group)):
            offset = sum((bit for k, bit in enumerate(group) if code >> k & 1))
            parts.append(lax.ppermute(data, axis_name, [(j, j ^ offset) for j in range(count)]))
        data = jnp.stack(parts)
    return data


def xor_parts(data, axis_name, group):
    count = lax.axis_size(axis_name)
    parts = [data]
    for code in range(1, 1 << len(group)):
        offset = sum((bit for k, bit in enumerate(group) if code >> k & 1))
        parts.append(lax.ppermute(data, axis_name, [(j, j ^ offset) for j in range(count)]))
    return parts


def stacked_position(offset, groups):
    position = jnp.zeros_like(offset)
    for group in reversed(groups):
        digit = sum((offset // bit % 2 << k for k, bit in enumerate(group)))
        position = position * (1 << len(group)) + digit
    return position


def bit_groups(bits):
    return [bits[k : k + 2] for k in range(0, len(bits), 2)]


def gather_operators(x_operator, y_operator, after):
    mem_count = lax.axis_size("mem")
    tile_count = lax.axis_size("tile")
    x_rows, x_cols = x_operator.shape
    y_rows, y_cols = y_operator.shape
    width = max(x_cols, y_cols)
    both = jnp.concatenate(
        [
            jnp.pad(x_operator, ((0, 0), (0, width - x_cols))),
            jnp.pad(y_operator, ((0, 0), (0, width - y_cols))),
        ]
    )
    mem_bits = bit_groups([1 << k for k in range(mem_count.bit_length() - 1)])
    tile_bits = bit_groups([1 << k for k in range(1, tile_count.bit_length() - 1)]) + [[1]]
    both = xor_gather(both, "mem", mem_bits)
    chip_groups = tile_bits[:-1]
    both = xor_gather(both, "tile", chip_groups[:-1])
    parts = xor_parts(both, "tile", chip_groups[-1]) if chip_groups else [both]
    parts, after = lax.optimization_barrier((parts, after))
    swapped = [
        lax.ppermute(part, "tile", [(j, j ^ 1) for j in range(tile_count)]) for part in parts
    ]
    both = jnp.stack([jnp.stack(parts), jnp.stack(swapped)])
    both = both.reshape(mem_count * tile_count, x_rows + y_rows, width)
    mem_of = lax.broadcasted_iota(jnp.int32, (mem_count, tile_count), 0)
    tile_of = lax.broadcasted_iota(jnp.int32, (mem_count, tile_count), 1)
    position = stacked_position(tile_of ^ lax.axis_index("tile"), tile_bits) * mem_count
    position = position + stacked_position(mem_of ^ lax.axis_index("mem"), mem_bits)
    position = position.reshape(-1)
    x_full = jnp.take(both[:, :x_rows, :x_cols], position, axis=0, mode="clip")
    y_full = jnp.take(both[:, x_rows:, :y_cols], position, axis=0, mode="clip")
    x_full = x_full.reshape(mem_count * tile_count * x_rows, x_cols)
    y_full = y_full.reshape(mem_count * tile_count * y_rows, y_cols)
    return (x_full, y_full, after)


def body(
    source_blocks, send_blocks, recv_slot, recv_weight, recv_count, regional, x_operator, y_operator
):
    tile_count = lax.axis_size("tile")
    member_count, level_count, columns, y_cells = regional.shape
    capacity = send_blocks.shape[2]
    block_cells = source_blocks.shape[3]
    block_side = math.isqrt(block_cells)
    picked = send_blocks[0].reshape(-1)
    held = source_blocks.shape[0]
    one_hot = (picked[:, None] == lax.broadcasted_iota(jnp.int32, (1, held), 1)).astype(
        source_blocks.dtype
    )
    packed = jnp.dot(
        one_hot, source_blocks.reshape(held, -1), preferred_element_type=jnp.float32
    ).astype(source_blocks.dtype)
    packed = packed.reshape(tile_count, capacity, -1)
    arrived = lax.all_to_all(packed, "tile", split_axis=0, concat_axis=0, tiled=True)
    slot_count = columns // block_side * (y_cells // block_side)
    live_mask = lax.broadcasted_iota(jnp.int32, (tile_count, capacity), 1) < recv_count[0][:, None]
    weights = jnp.where(live_mask, recv_weight[0], 0.0).reshape(-1)
    slot_match = recv_slot[0].reshape(-1)[None, :] == lax.broadcasted_iota(
        jnp.int32, (slot_count, tile_count * capacity), 0
    )
    remap_weights = jnp.where(slot_match, weights[None, :], 0.0).astype(jnp.bfloat16)
    remapped = jnp.dot(
        remap_weights,
        arrived.reshape(tile_count * capacity, -1),
        preferred_element_type=jnp.float32,
    )
    remapped = remapped.reshape(
        columns // block_side,
        y_cells // block_side,
        member_count,
        level_count,
        block_side,
        block_side,
    )
    remapped = remapped.transpose(2, 3, 0, 4, 1, 5).reshape(
        member_count, level_count, columns, y_cells
    )
    difference = (remapped - regional.astype(jnp.float32)).astype(jnp.bfloat16)
    x_full, y_full, difference = gather_operators(x_operator, y_operator, difference)
    x_lines = lax.all_to_all(difference, "tile", split_axis=3, concat_axis=2, tiled=True)
    after_first = jnp.einsum(
        "ax,mlxy->mlay", x_full, x_lines, preferred_element_type=jnp.float32
    ).astype(jnp.bfloat16)
    y_chunk = y_cells // tile_count
    outgoing = after_first.reshape(
        member_count, level_count, tile_count, columns, y_chunk
    ).transpose(2, 0, 1, 3, 4)
    tile_back = lax.all_to_all(outgoing, "tile", split_axis=0, concat_axis=0, tiled=True)
    after_second = jnp.einsum(
        "tmlxy,bty->mlxb",
        tile_back,
        y_full.reshape(y_cells, tile_count, y_chunk),
        preferred_element_type=jnp.float32,
    )
    return (regional.astype(jnp.float32) + after_second).astype(jnp.bfloat16)


def solution(mesh):
    placed = (
        P("tile", "mem", None, None),
        P("tile", None, None),
        P("tile", None, None),
        P("tile", None, None),
        P("tile", None),
        P("mem", None, "tile", None),
        P(("mem", "tile"), None),
        P(("mem", "tile"), None),
    )
    return jax.shard_map(
        body, mesh=mesh, in_specs=placed, out_specs=P("mem", None, "tile", None), check_vma=False
    )
```

profile of v0, /device:TPU:0, one launch (start us, length us, event | category | flops | bytes accessed | tf_op | source)
XLA Modules:
  0.0 54.1 jit_solution(3132020845288126406)
XLA Ops:
  0.0 0.8 %fusion.32 = (bf16[1,28,512]{2,1,0:T(8,128)(2,1)S(1)}, bf16[28,512]{1,0:T(8,128)(2,1)S(1)}) fusion(bf16[12,384]{1,0:T(8,128)(2,1)} %param.15, bf16[16,512]{1,0:T(8,128)(2,1)} %param.14), kind=kLoop, calls=%fused_computation.86 | loop fusion | flops 86016 | bytes 82944 | tf_op jit(solution)/shard_map/stack | solution.py:15
  0.8 3.0 %collective-permute-start = (bf16[28,512]{1,0:T(8,128)(2,1)S(1)}, bf16[28,512]{1,0:T(8,128)(2,1)S(1)}, u32[]{:S(2)}, u32[]{:S(2)}) collective-permute-start(bf16[28,512]{1,0:T(8,128)(2,1)S(1)} %get-tuple-element.16), channel_id=1, source_target_pairs={{0,8},{8,0},{16,24},{24,16},{1,9},{9,1},{17,25},{25,17},{2,10},{10... | collective-permute-start | bytes 86024 | tf_op jit(solution)/shard_map/ppermute | solution.py:14
  3.8 2.6 %collective-permute-start.1 = (bf16[28,512]{1,0:T(8,128)(2,1)S(1)}, bf16[28,512]{1,0:T(8,128)(2,1)S(1)}, u32[]{:S(2)}, u32[]{:S(2)}) collective-permute-start(bf16[28,512]{1,0:T(8,128)(2,1)S(1)} %get-tuple-element.16), channel_id=1, source_target_pairs={{0,16},{8,24},{16,0},{24,8},{1,17},{9,25},{17,1},{25,9},{2,18},{10... | collective-permute-start | bytes 86024 | tf_op jit(solution)/shard_map/ppermute | solution.py:14
  6.4 1.1 %reshape.467 = bf16[128,1024]{1,0:T(8,128)(2,1)S(1)} reshape(bf16[128,2,2,256]{3,2,1,0:T(2,128)(2,1)} %param.8) | data formatting | bytes 524288 | tf_op jit(solution)/shard_map/reshape | solution.py:90
  7.5 0.8 %eq.39 = s32[192]{0:T(256)S(1)} reshape(s32[1,8,24]{2,1,0:T(8,128)} %param.9) | data formatting | bytes 1536 | tf_op jit(solution)/shard_map/eq | solution.py:86
  8.3 1.1 %convolution_convert_fusion = bf16[192,1024]{1,0:T(8,128)(2,1)} fusion(bf16[128,1024]{1,0:T(8,128)(2,1)S(1)} %reshape.467, s32[192]{0:T(256)S(1)} %eq.39), kind=kOutput, calls=%fused_computation.3 | convolution fusion | flops 50552832 | bytes 656128 | tf_op jit(solution)/shard_map/dot_general | solution.py:89
  9.4 3.9 %all-to-all-start = ((bf16[8,24,1024]{2,1,0:T(8,128)(2,1)}), bf16[8,24,1024]{2,1,0:T(8,128)(2,1)S(1)}, u32[]{:S(2)}, u32[]{:S(2)}) async-start(bf16[8,24,1024]{2,1,0:T(8,128)(2,1)} %bitcast.7), calls=%async_computation | async-start | bytes 786432 | tf_op jit(solution)/shard_map/all_to_all | solution.py:93
  14.4 0.7 %pad_maximum_fusion.1 = bf16[4,28,512]{2,1,0:T(8,128)(2,1)} fusion(bf16[1,28,512]{2,1,0:T(8,128)(2,1)S(1)} %bitcast.94, bf16[1,28,512]{2,1,0:T(8,128)(2,1)S(1)} %bitcast.93, bf16[1,28,512]{2,1,0:T(8,128)(2,1)S(1)} %bitcast.92, bf16[1,28,512]{2,1,0:T(8,128)(2,1)S(1)} %get-tuple-element.15), kind=kLoop, calls=%fused_computation.18 | loop fusion | flops 172032 | bytes 229376 | tf_op jit(solution)/shard_map/stack | solution.py:15
  15.1 2.0 %collective-permute-start.3 = (bf16[4,28,512]{2,1,0:T(8,128)(2,1)}, bf16[4,28,512]{2,1,0:T(8,128)(2,1)}, u32[]{:S(2)}, u32[]{:S(2)}) collective-permute-start(bf16[4,28,512]{2,1,0:T(8,128)(2,1)} %pad_maximum_fusion.1), channel_id=1, source_target_pairs={{0,2},{1,3},{2,0},{3,1},{4,6},{5,7},{6,4},{7,5},{8,10},{9,11},{10,... | collective-permute-start | bytes 344072 | tf_op jit(solution)/shard_map/ppermute | solution.py:24
  17.1 1.5 %collective-permute-start.4 = (bf16[4,28,512]{2,1,0:T(8,128)(2,1)}, bf16[4,28,512]{2,1,0:T(8,128)(2,1)}, u32[]{:S(2)}, u32[]{:S(2)}) collective-permute-start(bf16[4,28,512]{2,1,0:T(8,128)(2,1)} %pad_maximum_fusion.1), channel_id=1, source_target_pairs={{0,4},{1,5},{2,6},{3,7},{4,0},{5,1},{6,2},{7,3},{8,12},{9,13},{10,... | collective-permute-start | bytes 344072 | tf_op jit(solution)/shard_map/ppermute | solution.py:24
  18.6 3.5 %all-to-all-done = bf16[8,24,1024]{2,1,0:T(8,128)(2,1)S(1)} async-done(((bf16[8,24,1024]{2,1,0:T(8,128)(2,1)}), bf16[8,24,1024]{2,1,0:T(8,128)(2,1)S(1)}, u32[]{:S(2)}, u32[]{:S(2)}) %all-to-all-start) | async-done | bytes 393248 | tf_op jit(solution)/shard_map/all_to_all | solution.py:93
  22.3 1.9 %convolution_bitcast_fusion = f32[2,2,4,16,24,16]{4,5,3,1,0,2:T(8,128)} fusion(bf16[2,2,16,16,192,1]{4,3,2,1,0,5:T(8,128)(2,1)S(1)} %bitcast.81, bf16[192]{0:T(256)(128)(2,1)S(1)} %broadcast_select_fusion.3, s32[4,24]{1,0:T(4,128)S(1)} %multiply_add_fusion, s32[192]{0:T(256)S(1)} %eq.36), kind=kOutput, calls=%fused_computation.2 | convolution fusion | flops 37785600 | bytes 787968 | tf_op jit(solution)/shard_map/dot_general | solution.py:101
  24.2 2.2 %copy.19 = f32[2,2,4,16,24,16]{5,4,3,2,1,0:T(8,128)S(1)} copy(f32[2,2,4,16,24,16]{4,5,3,1,0,2:T(8,128)} %convolution_bitcast_fusion) | data formatting | bytes 786432 | tf_op jit(solution)/shard_map/transpose | solution.py:114
  26.4 0.9 %reshape.470 = f32[2,2,64,384]{3,2,1,0:T(8,128)S(1)} reshape(f32[2,2,4,16,24,16]{5,4,3,2,1,0:T(8,128)S(1)} %copy.19) | data formatting | bytes 786432 | tf_op jit(solution)/shard_map/reshape | solution.py:114
  27.3 1.0 %fusion.3 = bf16[2,2,64,384]{3,2,1,0:T(8,128)(2,1)S(1)} fusion(f32[2,2,64,384]{3,2,1,0:T(8,128)S(1)} %reshape.470, bf16[2,2,64,384]{3,2,1,0:T(8,128)(2,1)} %param.13), kind=kLoop, calls=%fused_computation.13 | loop fusion | flops 294912 | bytes 786432 | tf_op jit(solution)/shard_map/convert_element_type | solution.py:117
  30.0 1.0 %reshape.495 = bf16[8,2,6144]{2,1,0:T(2,128)(2,1)} reshape(bf16[384,2,2,64]{3,2,1,0:T(2,128)(2,1)S(1)} %bitcast.83) | data formatting | bytes 393216
  31.0 3.4 %all-to-all-start.1 = ((bf16[8,2,6144]{2,1,0:T(2,128)(2,1)}), bf16[8,2,6144]{2,1,0:T(2,128)(2,1)S(1)}, u32[]{:S(2)}, u32[]{:S(2)}) async-start(bf16[8,2,6144]{2,1,0:T(2,128)(2,1)} %reshape.495), calls=%async_computation.1 | async-start | bytes 393216 | tf_op jit(solution)/shard_map/all_to_all | solution.py:119
  34.4 1.2 %maximum_bitcast_fusion = bf16[1,4,4,28,512]{4,3,2,1,0:T(8,128)(2,1)S(1)} fusion(bf16[1,4,28,512]{3,2,1,0:T(8,128)(2,1)} %bitcast.19, bf16[1,4,28,512]{3,2,1,0:T(8,128)(2,1)} %bitcast.18, bf16[1,4,28,512]{3,2,1,0:T(8,128)(2,1)} %bitcast.17, bf16[1,4,28,512]{3,2,1,0:T(8,128)(2,1)} %bitcast.16), kind=kLoop, calls=%fused_computation.9 | loop fusion | flops 688128 | bytes 917504 | tf_op jit(solution)/shard_map/stack | solution.py:62
  36.4 4.1 %all-to-all-done.1 = bf16[8,2,6144]{2,1,0:T(2,128)(2,1)S(1)} async-done(((bf16[8,2,6144]{2,1,0:T(2,128)(2,1)}), bf16[8,2,6144]{2,1,0:T(2,128)(2,1)S(1)}, u32[]{:S(2)}, u32[]{:S(2)}) %all-to-all-start.1) | async-done | bytes 196640 | tf_op jit(solution)/shard_map/all_to_all | solution.py:119
  42.0 1.0 %reshape.497 = bf16[8,2,6144]{2,1,0:T(2,128)(2,1)} reshape(bf16[8,2,2,48,64]{4,3,2,1,0:T(8,128)(2,1)S(1)} %bitcast.86) | data formatting | bytes 393216
  43.0 3.4 %all-to-all-start.2 = ((bf16[8,2,6144]{2,1,0:T(2,128)(2,1)}), bf16[8,2,6144]{2,1,0:T(2,128)(2,1)S(1)}, u32[]{:S(2)}, u32[]{:S(2)}) async-start(bf16[8,2,6144]{2,1,0:T(2,128)(2,1)} %reshape.497), calls=%async_computation.2 | async-start | bytes 393216 | tf_op jit(solution)/shard_map/all_to_all | solution.py:127
  47.1 0.7 %reshape_reshape.3 = bf16[384,8,48]{2,1,0:T(8,128)(2,1)S(1)} reshape(bf16[32,12,384]{2,1,0:T(8,128)(2,1)S(1)} %gather_fusion.1) | data formatting | bytes 589824 | tf_op jit(solution)/shard_map/reshape;reshape | solution.py:131
  47.8 4.8 %all-to-all-done.2 = bf16[8,2,6144]{2,1,0:T(2,128)(2,1)S(1)} async-done(((bf16[8,2,6144]{2,1,0:T(2,128)(2,1)}), bf16[8,2,6144]{2,1,0:T(2,128)(2,1)S(1)}, u32[]{:S(2)}, u32[]{:S(2)}) %all-to-all-start.2) | async-done | bytes 196640 | tf_op jit(solution)/shard_map/all_to_all | solution.py:127
  53.4 0.7 %fusion.4 = bf16[2,2,64,384]{3,2,1,0:T(8,128)(2,1)} fusion(bf16[2,2,64,384]{3,2,1,0:T(8,128)(2,1)S(1)} %copy-done, f32[2,2,64,384,1]{3,2,0,1,4:T(8,128)S(1)} %fusion.1), kind=kLoop, calls=%fused_computation.14 | loop fusion | flops 294912 | bytes 786432 | tf_op jit(solution)/shard_map/convert_element_type | solution.py:134
  (65 shorter events, 6.6 us)
Async XLA Ops:
  0.0 13.4 %copy-start.3 = (s32[1,8]{1,0:T(1,128)S(1)}, s32[1,8]{1,0:T(1,128)}, u32[]{:S(2)}) copy-start(s32[1,8]{1,0:T(1,128)} %param.12) | copy-start | bytes 100
  0.0 13.6 %copy-start.2 = (f32[1,8,24]{2,1,0:T(8,128)S(1)}, f32[1,8,24]{2,1,0:T(8,128)}, u32[]{:S(2)}) copy-start(f32[1,8,24]{2,1,0:T(8,128)} %param.11) | copy-start | bytes 2308
  0.0 14.3 %copy-start.1 = (s32[1,8,24]{2,1,0:T(8,128)S(1)}, s32[1,8,24]{2,1,0:T(8,128)}, u32[]{:S(2)}) copy-start(s32[1,8,24]{2,1,0:T(8,128)} %param.10) | copy-start | bytes 2308
  0.8 13.6 %collective-permute-start = (bf16[28,512]{1,0:T(8,128)(2,1)S(1)}, bf16[28,512]{1,0:T(8,128)(2,1)S(1)}, u32[]{:S(2)}, u32[]{:S(2)}) collective-permute-start(bf16[28,512]{1,0:T(8,128)(2,1)S(1)} %get-tuple-element.16), channel_id=1, source_target_pairs={{0,8},{8,0},{16,24},{24,16},{1,9},{9,1},{17,25},{25,17},{2,10},{10... | collective-permute-start | bytes 86024 | tf_op jit(solution)/shard_map/ppermute | solution.py:14
  3.8 10.6 %collective-permute-start.1 = (bf16[28,512]{1,0:T(8,128)(2,1)S(1)}, bf16[28,512]{1,0:T(8,128)(2,1)S(1)}, u32[]{:S(2)}, u32[]{:S(2)}) collective-permute-start(bf16[28,512]{1,0:T(8,128)(2,1)S(1)} %get-tuple-element.16), channel_id=1, source_target_pairs={{0,16},{8,24},{16,0},{24,8},{1,17},{9,25},{17,1},{25,9},{2,18},{10... | collective-permute-start | bytes 86024 | tf_op jit(solution)/shard_map/ppermute | solution.py:14
  6.4 8.0 %collective-permute-start.2 = (bf16[28,512]{1,0:T(8,128)(2,1)S(1)}, bf16[28,512]{1,0:T(8,128)(2,1)S(1)}, u32[]{:S(2)}, u32[]{:S(2)}) collective-permute-start(bf16[28,512]{1,0:T(8,128)(2,1)S(1)} %get-tuple-element.16), channel_id=1, source_target_pairs={{0,24},{8,16},{16,8},{24,0},{1,25},{9,17},{17,9},{25,1},{2,26},{10... | collective-permute-start | bytes 86024 | tf_op jit(solution)/shard_map/ppermute | solution.py:14
  9.4 12.8 %all-to-all-start = ((bf16[8,24,1024]{2,1,0:T(8,128)(2,1)}), bf16[8,24,1024]{2,1,0:T(8,128)(2,1)S(1)}, u32[]{:S(2)}, u32[]{:S(2)}) async-start(bf16[8,24,1024]{2,1,0:T(8,128)(2,1)} %bitcast.7), calls=%async_computation | async-start | bytes 786432 | tf_op jit(solution)/shard_map/all_to_all | solution.py:93
  15.1 13.2 %collective-permute-start.3 = (bf16[4,28,512]{2,1,0:T(8,128)(2,1)}, bf16[4,28,512]{2,1,0:T(8,128)(2,1)}, u32[]{:S(2)}, u32[]{:S(2)}) collective-permute-start(bf16[4,28,512]{2,1,0:T(8,128)(2,1)} %pad_maximum_fusion.1), channel_id=1, source_target_pairs={{0,2},{1,3},{2,0},{3,1},{4,6},{5,7},{6,4},{7,5},{8,10},{9,11},{10,... | collective-permute-start | bytes 344072 | tf_op jit(solution)/shard_map/ppermute | solution.py:24
  17.1 11.2 %collective-permute-start.4 = (bf16[4,28,512]{2,1,0:T(8,128)(2,1)}, bf16[4,28,512]{2,1,0:T(8,128)(2,1)}, u32[]{:S(2)}, u32[]{:S(2)}) collective-permute-start(bf16[4,28,512]{2,1,0:T(8,128)(2,1)} %pad_maximum_fusion.1), channel_id=1, source_target_pairs={{0,4},{1,5},{2,6},{3,7},{4,0},{5,1},{6,2},{7,3},{8,12},{9,13},{10,... | collective-permute-start | bytes 344072 | tf_op jit(solution)/shard_map/ppermute | solution.py:24
  18.6 9.7 %collective-permute-start.5 = (bf16[4,28,512]{2,1,0:T(8,128)(2,1)}, bf16[4,28,512]{2,1,0:T(8,128)(2,1)}, u32[]{:S(2)}, u32[]{:S(2)}) collective-permute-start(bf16[4,28,512]{2,1,0:T(8,128)(2,1)} %pad_maximum_fusion.1), channel_id=1, source_target_pairs={{0,6},{1,7},{2,4},{3,5},{4,2},{5,3},{6,0},{7,1},{8,14},{9,15},{10,... | collective-permute-start | bytes 344072 | tf_op jit(solution)/shard_map/ppermute | solution.py:24
  28.3 7.3 %collective-permute-start.6 = (bf16[4,28,512]{2,1,0:T(8,128)(2,1)}, bf16[4,28,512]{2,1,0:T(8,128)(2,1)S(1)}, u32[]{:S(2)}, u32[]{:S(2)}) collective-permute-start(bf16[4,28,512]{2,1,0:T(8,128)(2,1)} %pad_maximum_fusion.1), channel_id=1, source_target_pairs={{0,1},{1,0},{2,3},{3,2},{4,5},{5,4},{6,7},{7,6},{8,9},{9,8},{10,11... | collective-permute-start | bytes 344072 | tf_op jit(solution)/shard_map/ppermute | solution.py:60
  28.4 7.2 %collective-permute-start.7 = (bf16[4,28,512]{2,1,0:T(8,128)(2,1)}, bf16[4,28,512]{2,1,0:T(8,128)(2,1)S(1)}, u32[]{:S(2)}, u32[]{:S(2)}) collective-permute-start(bf16[4,28,512]{2,1,0:T(8,128)(2,1)} %collective-permute-done.3), channel_id=1, source_target_pairs={{0,1},{1,0},{2,3},{3,2},{4,5},{5,4},{6,7},{7,6},{8,9},{9,8},{10,11... | collective-permute-start | bytes 344072 | tf_op jit(solution)/shard_map/ppermute | solution.py:60
  28.9 6.7 %collective-permute-start.8 = (bf16[4,28,512]{2,1,0:T(8,128)(2,1)}, bf16[4,28,512]{2,1,0:T(8,128)(2,1)S(1)}, u32[]{:S(2)}, u32[]{:S(2)}) collective-permute-start(bf16[4,28,512]{2,1,0:T(8,128)(2,1)} %collective-permute-done.4), channel_id=1, source_target_pairs={{0,1},{1,0},{2,3},{3,2},{4,5},{5,4},{6,7},{7,6},{8,9},{9,8},{10,11... | collective-permute-start | bytes 344072 | tf_op jit(solution)/shard_map/ppermute | solution.py:60
  29.0 6.6 %collective-permute-start.9 = (bf16[4,28,512]{2,1,0:T(8,128)(2,1)}, bf16[4,28,512]{2,1,0:T(8,128)(2,1)S(1)}, u32[]{:S(2)}, u32[]{:S(2)}) collective-permute-start(bf16[4,28,512]{2,1,0:T(8,128)(2,1)} %collective-permute-done.5), channel_id=1, source_target_pairs={{0,1},{1,0},{2,3},{3,2},{4,5},{5,4},{6,7},{7,6},{8,9},{9,8},{10,11... | collective-permute-start | bytes 344072 | tf_op jit(solution)/shard_map/ppermute | solution.py:60
  31.0 9.6 %all-to-all-start.1 = ((bf16[8,2,6144]{2,1,0:T(2,128)(2,1)}), bf16[8,2,6144]{2,1,0:T(2,128)(2,1)S(1)}, u32[]{:S(2)}, u32[]{:S(2)}) async-start(bf16[8,2,6144]{2,1,0:T(2,128)(2,1)} %reshape.495), calls=%async_computation.1 | async-start | bytes 393216 | tf_op jit(solution)/shard_map/all_to_all | solution.py:119
  43.0 9.6 %all-to-all-start.2 = ((bf16[8,2,6144]{2,1,0:T(2,128)(2,1)}), bf16[8,2,6144]{2,1,0:T(2,128)(2,1)S(1)}, u32[]{:S(2)}, u32[]{:S(2)}) async-start(bf16[8,2,6144]{2,1,0:T(2,128)(2,1)} %reshape.497), calls=%async_computation.2 | async-start | bytes 393216 | tf_op jit(solution)/shard_map/all_to_all | solution.py:127
  46.4 6.9 %copy-start = (bf16[2,2,64,384]{3,2,1,0:T(8,128)(2,1)S(1)}, bf16[2,2,64,384]{3,2,1,0:T(8,128)(2,1)}, u32[]{:S(2)}) copy-start(bf16[2,2,64,384]{3,2,1,0:T(8,128)(2,1)} %param.13) | copy-start | bytes 589828
where the time goes:
time: 54.7 us; the launch traced here: 54.1 us
  starting transfers between devices  20.9 us (38%)
  waiting for transfers between devices  12.4 us (23%)
  local copies, waits for them, and re-layouts  11.9 us (22%)
  other arithmetic  4.78 us (9%)
  matrix products  3.76 us (7%)
    ppermute x3, starting transfers between devices, xor_gather(): lax.ppermute(data, axis_name, [(j, j ^ offset) for j in range(count)])  5.62 us
    all_to_all x1, waiting for transfers between devices, body(): lax.all_to_all(outgoing, 'tile', split_axis=0, concat_axis=0, tiled=True)  4.76 us
    all_to_all x1, waiting for transfers between devices, body(): lax.all_to_all(difference, 'tile', split_axis=3, concat_axis=2, tiled=True)  4.11 us
    all_to_all x1, starting transfers between devices, body(): lax.all_to_all(packed, 'tile', split_axis=0, concat_axis=0, tiled=True)  3.94 us
    all_to_all x1, waiting for transfers between devices, body(): lax.all_to_all(packed, 'tile', split_axis=0, concat_axis=0, tiled=True)  3.5 us
    ppermute x3, starting transfers between devices, xor_parts(): lax.ppermute(data, axis_name, [(j, j ^ offset) for j in range(count)])  3.49 us
    all_to_all x1, starting transfers between devices, body(): lax.all_to_all(difference, 'tile', split_axis=3, concat_axis=2, tiled=True)  3.39 us
    all_to_all x1, starting transfers between devices, body(): lax.all_to_all(outgoing, 'tile', split_axis=0, concat_axis=0, tiled=True)  3.39 us
  transfers between devices with their start and end apart: 13, of which 3 were waited for; matrix products, arithmetic and copies ran while one was open for 29% of the time, Pallas kernels for 0%

commit v1 on v0

--- a/solution.py
+++ b/solution.py
@@ -116,7 +116,12 @@
     )
     difference = (remapped - regional.astype(jnp.float32)).astype(jnp.bfloat16)
     x_full, y_full, difference = gather_operators(x_operator, y_operator, difference)
-    x_lines = lax.all_to_all(difference, "tile", split_axis=3, concat_axis=2, tiled=True)
+    x_lines = jnp.concatenate(
+        lax.all_to_all(
+            jnp.stack(jnp.split(difference, lax.axis_size("tile"), axis=3)), "tile", 0, 0
+        ),
+        axis=2,
+    )
     after_first = jnp.einsum(
         "ax,mlxy->mlay", x_full, x_lines, preferred_element_type=jnp.float32
     ).astype(jnp.bfloat16)

time: 54.7 us -> 54 us (0.987)
  waiting for transfers between devices: 12.4 us -> 11.3 us
    all_to_all x1, waiting for transfers between devices: 4.11 us -> 2.86 us  [body(): lax.all_to_all(jnp.stack(jnp.split(difference, lax.axis_size('tile'), axi...]
    unnamed x12 -> x19, local copies, waits for them, and re-layouts: 2.56 us -> 3.18 us
    optimization_barrier x1 -> x0, local copies, waits for them, and re-layouts: 0.59 us -> none  [gather_operators(): parts, after = lax.optimization_barrier((parts, after))]
  transfers between devices with their start and end apart: 13 -> 13, of which waited for: 3 -> 4; matrix products, arithmetic and copies ran while one was open for 29% -> 26% of each run, Pallas kernels for 0% -> 0%
where the time goes in v1:
time: 54 us; the launch traced here: 53.4 us
  starting transfers between devices  20.9 us (39%)
  local copies, waits for them, and re-layouts  12.3 us (23%)
  waiting for transfers between devices  11.3 us (21%)
  other arithmetic  4.77 us (9%)
  matrix products  3.76 us (7%)
    ppermute x3, starting transfers between devices, xor_gather(): lax.ppermute(data, axis_name, [(j, j ^ offset) for j in range(count)])  5.62 us
    all_to_all x1, waiting for transfers between devices, body(): lax.all_to_all(outgoing, 'tile', split_axis=0, concat_axis=0, tiled=True)  4.76 us
    all_to_all x1, starting transfers between devices, body(): lax.all_to_all(packed, 'tile', split_axis=0, concat_axis=0, tiled=True)  3.94 us
    all_to_all x1, waiting for transfers between devices, body(): lax.all_to_all(packed, 'tile', split_axis=0, concat_axis=0, tiled=True)  3.5 us
    ppermute x3, starting transfers between devices, xor_parts(): lax.ppermute(data, axis_name, [(j, j ^ offset) for j in range(count)])  3.49 us
    all_to_all x1, starting transfers between devices, body(): lax.all_to_all(jnp.stack(jnp.split(difference, lax.axis_size('tile'), axi...  3.39 us
    all_to_all x1, starting transfers between devices, body(): lax.all_to_all(outgoing, 'tile', split_axis=0, concat_axis=0, tiled=True)  3.39 us
    unnamed x19, local copies, waits for them, and re-layouts  3.18 us
  transfers between devices with their start and end apart: 13, of which 4 were waited for; matrix products, arithmetic and copies ran while one was open for 26% of the time, Pallas kernels for 0%

profile of v1, /device:TPU:0, one launch (start us, length us, event | category | flops | bytes accessed | tf_op | source)
XLA Modules:
  0.0 53.4 jit_solution(7524736896458462390)
XLA Ops:
  0.0 0.8 %fusion.32 = (bf16[1,28,512]{2,1,0:T(8,128)(2,1)S(1)}, bf16[28,512]{1,0:T(8,128)(2,1)S(1)}) fusion(bf16[12,384]{1,0:T(8,128)(2,1)} %param.15, bf16[16,512]{1,0:T(8,128)(2,1)} %param.14), kind=kLoop, calls=%fused_computation.93 | loop fusion | flops 86016 | bytes 82944 | tf_op jit(solution)/shard_map/stack | solution.py:15
  0.8 3.0 %collective-permute-start = (bf16[28,512]{1,0:T(8,128)(2,1)S(1)}, bf16[28,512]{1,0:T(8,128)(2,1)S(1)}, u32[]{:S(2)}, u32[]{:S(2)}) collective-permute-start(bf16[28,512]{1,0:T(8,128)(2,1)S(1)} %get-tuple-element.16), channel_id=1, source_target_pairs={{0,8},{8,0},{16,24},{24,16},{1,9},{9,1},{17,25},{25,17},{2,10},{10... | collective-permute-start | bytes 86024 | tf_op jit(solution)/shard_map/ppermute | solution.py:14
  3.8 2.6 %collective-permute-start.1 = (bf16[28,512]{1,0:T(8,128)(2,1)S(1)}, bf16[28,512]{1,0:T(8,128)(2,1)S(1)}, u32[]{:S(2)}, u32[]{:S(2)}) collective-permute-start(bf16[28,512]{1,0:T(8,128)(2,1)S(1)} %get-tuple-element.16), channel_id=1, source_target_pairs={{0,16},{8,24},{16,0},{24,8},{1,17},{9,25},{17,1},{25,9},{2,18},{10... | collective-permute-start | bytes 86024 | tf_op jit(solution)/shard_map/ppermute | solution.py:14
  6.4 1.1 %reshape.473 = bf16[128,1024]{1,0:T(8,128)(2,1)S(1)} reshape(bf16[128,2,2,256]{3,2,1,0:T(2,128)(2,1)} %param.8) | data formatting | bytes 524288 | tf_op jit(solution)/shard_map/reshape | solution.py:90
  7.5 0.8 %eq.39 = s32[192]{0:T(256)S(1)} reshape(s32[1,8,24]{2,1,0:T(8,128)} %param.9) | data formatting | bytes 1536 | tf_op jit(solution)/shard_map/eq | solution.py:86
  8.3 1.1 %convolution_convert_fusion = bf16[192,1024]{1,0:T(8,128)(2,1)} fusion(bf16[128,1024]{1,0:T(8,128)(2,1)S(1)} %reshape.473, s32[192]{0:T(256)S(1)} %eq.39), kind=kOutput, calls=%fused_computation.3 | convolution fusion | flops 50552832 | bytes 656128 | tf_op jit(solution)/shard_map/dot_general | solution.py:89
  9.4 3.9 %all-to-all-start = ((bf16[8,24,1024]{2,1,0:T(8,128)(2,1)}), bf16[8,24,1024]{2,1,0:T(8,128)(2,1)S(1)}, u32[]{:S(2)}, u32[]{:S(2)}) async-start(bf16[8,24,1024]{2,1,0:T(8,128)(2,1)} %bitcast.7), calls=%async_computation | async-start | bytes 786432 | tf_op jit(solution)/shard_map/all_to_all | solution.py:93
  14.4 0.7 %pad_maximum_fusion.1 = bf16[4,28,512]{2,1,0:T(8,128)(2,1)} fusion(bf16[1,28,512]{2,1,0:T(8,128)(2,1)S(1)} %bitcast.106, bf16[1,28,512]{2,1,0:T(8,128)(2,1)S(1)} %bitcast.105, bf16[1,28,512]{2,1,0:T(8,128)(2,1)S(1)} %bitcast.104, bf16[1,28,512]{2,1,0:T(8,128)(2,1)S(1)} %get-tuple-element.15), kind=kLoop, calls=%fused_computation.17 | loop fusion | flops 172032 | bytes 229376 | tf_op jit(solution)/shard_map/stack | solution.py:15
  15.1 2.0 %collective-permute-start.3 = (bf16[4,28,512]{2,1,0:T(8,128)(2,1)}, bf16[4,28,512]{2,1,0:T(8,128)(2,1)}, u32[]{:S(2)}, u32[]{:S(2)}) collective-permute-start(bf16[4,28,512]{2,1,0:T(8,128)(2,1)} %pad_maximum_fusion.1), channel_id=1, source_target_pairs={{0,2},{1,3},{2,0},{3,1},{4,6},{5,7},{6,4},{7,5},{8,10},{9,11},{10,... | collective-permute-start | bytes 344072 | tf_op jit(solution)/shard_map/ppermute | solution.py:24
  17.1 1.5 %collective-permute-start.4 = (bf16[4,28,512]{2,1,0:T(8,128)(2,1)}, bf16[4,28,512]{2,1,0:T(8,128)(2,1)}, u32[]{:S(2)}, u32[]{:S(2)}) collective-permute-start(bf16[4,28,512]{2,1,0:T(8,128)(2,1)} %pad_maximum_fusion.1), channel_id=1, source_target_pairs={{0,4},{1,5},{2,6},{3,7},{4,0},{5,1},{6,2},{7,3},{8,12},{9,13},{10,... | collective-permute-start | bytes 344072 | tf_op jit(solution)/shard_map/ppermute | solution.py:24
  18.6 3.5 %all-to-all-done = bf16[8,24,1024]{2,1,0:T(8,128)(2,1)S(1)} async-done(((bf16[8,24,1024]{2,1,0:T(8,128)(2,1)}), bf16[8,24,1024]{2,1,0:T(8,128)(2,1)S(1)}, u32[]{:S(2)}, u32[]{:S(2)}) %all-to-all-start) | async-done | bytes 393248 | tf_op jit(solution)/shard_map/all_to_all | solution.py:93
  22.3 1.9 %convolution_bitcast_fusion = f32[2,2,4,16,24,16]{4,5,3,1,0,2:T(8,128)} fusion(bf16[2,2,16,16,192,1]{4,3,2,1,0,5:T(8,128)(2,1)S(1)} %bitcast.95, bf16[192]{0:T(256)(128)(2,1)S(1)} %broadcast_select_fusion.3, s32[4,24]{1,0:T(4,128)S(1)} %multiply_add_fusion, s32[192]{0:T(256)S(1)} %eq.36), kind=kOutput, calls=%fused_computation.2 | convolution fusion | flops 37785600 | bytes 787968 | tf_op jit(solution)/shard_map/dot_general | solution.py:101
  24.2 2.2 %copy.19 = f32[2,2,4,16,24,16]{5,4,3,2,1,0:T(8,128)S(1)} copy(f32[2,2,4,16,24,16]{4,5,3,1,0,2:T(8,128)} %convolution_bitcast_fusion) | data formatting | bytes 786432 | tf_op jit(solution)/shard_map/transpose | solution.py:114
  26.4 0.9 %reshape.476 = f32[2,2,64,384]{3,2,1,0:T(8,128)S(1)} reshape(f32[2,2,4,16,24,16]{5,4,3,2,1,0:T(8,128)S(1)} %copy.19) | data formatting | bytes 786432 | tf_op jit(solution)/shard_map/reshape | solution.py:114
  27.3 1.0 %fusion.3 = bf16[2,2,64,384]{3,2,1,0:T(8,128)(2,1)S(1)} fusion(f32[2,2,64,384]{3,2,1,0:T(8,128)S(1)} %reshape.476, bf16[2,2,64,384]{3,2,1,0:T(8,128)(2,1)} %param.13), kind=kLoop, calls=%fused_computation.13 | loop fusion | flops 294912 | bytes 786432 | tf_op jit(solution)/shard_map/convert_element_type | solution.py:117
  29.3 1.0 %reshape.503 = bf16[8,2,6144]{2,1,0:T(2,128)(2,1)} reshape(bf16[8,2,2,48,64]{4,3,2,1,0:T(8,128)(2,1)S(1)} %bitcast.97) | data formatting | bytes 393216
  30.3 3.4 %all-to-all-start.1 = ((bf16[8,2,6144]{2,1,0:T(2,128)(2,1)}), bf16[8,2,6144]{2,1,0:T(2,128)(2,1)S(1)}, u32[]{:S(2)}, u32[]{:S(2)}) async-start(bf16[8,2,6144]{2,1,0:T(2,128)(2,1)} %reshape.503), calls=%async_computation.1 | async-start | bytes 393216 | tf_op jit(solution)/shard_map/all_to_all | solution.py:120
  34.8 1.2 %maximum_bitcast_fusion = bf16[1,4,4,28,512]{4,3,2,1,0:T(8,128)(2,1)S(1)} fusion(bf16[1,4,28,512]{3,2,1,0:T(8,128)(2,1)} %bitcast.25, bf16[1,4,28,512]{3,2,1,0:T(8,128)(2,1)} %bitcast.24, bf16[1,4,28,512]{3,2,1,0:T(8,128)(2,1)} %bitcast.23, bf16[1,4,28,512]{3,2,1,0:T(8,128)(2,1)} %bitcast.22), kind=kLoop, calls=%fused_computation.9 | loop fusion | flops 688128 | bytes 917504 | tf_op jit(solution)/shard_map/stack | solution.py:62
  37.0 2.9 %all-to-all-done.1 = bf16[8,2,6144]{2,1,0:T(2,128)(2,1)S(1)} async-done(((bf16[8,2,6144]{2,1,0:T(2,128)(2,1)}), bf16[8,2,6144]{2,1,0:T(2,128)(2,1)S(1)}, u32[]{:S(2)}, u32[]{:S(2)}) %all-to-all-start.1) | async-done | bytes 196640 | tf_op jit(solution)/shard_map/all_to_all | solution.py:120
  41.4 1.0 %reshape.505 = bf16[8,2,6144]{2,1,0:T(2,128)(2,1)} reshape(bf16[8,2,2,48,64]{4,3,2,1,0:T(8,128)(2,1)S(1)} %bitcast.98) | data formatting | bytes 393216
  42.3 3.4 %all-to-all-start.2 = ((bf16[8,2,6144]{2,1,0:T(2,128)(2,1)}), bf16[8,2,6144]{2,1,0:T(2,128)(2,1)S(1)}, u32[]{:S(2)}, u32[]{:S(2)}) async-start(bf16[8,2,6144]{2,1,0:T(2,128)(2,1)} %reshape.505), calls=%async_computation.2 | async-start | bytes 393216 | tf_op jit(solution)/shard_map/all_to_all | solution.py:132
  46.4 0.7 %reshape_reshape.3 = bf16[384,8,48]{2,1,0:T(8,128)(2,1)S(1)} reshape(bf16[32,12,384]{2,1,0:T(8,128)(2,1)S(1)} %gather_fusion.1) | data formatting | bytes 589824 | tf_op jit(solution)/shard_map/reshape;reshape | solution.py:136
  47.1 4.8 %all-to-all-done.2 = bf16[8,2,6144]{2,1,0:T(2,128)(2,1)S(1)} async-done(((bf16[8,2,6144]{2,1,0:T(2,128)(2,1)}), bf16[8,2,6144]{2,1,0:T(2,128)(2,1)S(1)}, u32[]{:S(2)}, u32[]{:S(2)}) %all-to-all-start.2) | async-done | bytes 196640 | tf_op jit(solution)/shard_map/all_to_all | solution.py:132
  52.7 0.7 %fusion.4 = bf16[2,2,64,384]{3,2,1,0:T(8,128)(2,1)} fusion(bf16[2,2,64,384]{3,2,1,0:T(8,128)(2,1)S(1)} %copy-done, f32[2,2,64,384,1]{3,2,0,1,4:T(8,128)S(1)} %fusion.1), kind=kLoop, calls=%fused_computation.14 | loop fusion | flops 294912 | bytes 786432 | tf_op jit(solution)/shard_map/convert_element_type | solution.py:139
  (74 shorter events, 7.2 us)
Async XLA Ops:
  0.0 13.4 %copy-start.3 = (s32[1,8]{1,0:T(1,128)S(1)}, s32[1,8]{1,0:T(1,128)}, u32[]{:S(2)}) copy-start(s32[1,8]{1,0:T(1,128)} %param.12) | copy-start | bytes 100
  0.0 13.6 %copy-start.2 = (f32[1,8,24]{2,1,0:T(8,128)S(1)}, f32[1,8,24]{2,1,0:T(8,128)}, u32[]{:S(2)}) copy-start(f32[1,8,24]{2,1,0:T(8,128)} %param.11) | copy-start | bytes 2308
  0.0 14.3 %copy-start.1 = (s32[1,8,24]{2,1,0:T(8,128)S(1)}, s32[1,8,24]{2,1,0:T(8,128)}, u32[]{:S(2)}) copy-start(s32[1,8,24]{2,1,0:T(8,128)} %param.10) | copy-start | bytes 2308
  0.8 13.6 %collective-permute-start = (bf16[28,512]{1,0:T(8,128)(2,1)S(1)}, bf16[28,512]{1,0:T(8,128)(2,1)S(1)}, u32[]{:S(2)}, u32[]{:S(2)}) collective-permute-start(bf16[28,512]{1,0:T(8,128)(2,1)S(1)} %get-tuple-element.16), channel_id=1, source_target_pairs={{0,8},{8,0},{16,24},{24,16},{1,9},{9,1},{17,25},{25,17},{2,10},{10... | collective-permute-start | bytes 86024 | tf_op jit(solution)/shard_map/ppermute | solution.py:14
  3.8 10.6 %collective-permute-start.1 = (bf16[28,512]{1,0:T(8,128)(2,1)S(1)}, bf16[28,512]{1,0:T(8,128)(2,1)S(1)}, u32[]{:S(2)}, u32[]{:S(2)}) collective-permute-start(bf16[28,512]{1,0:T(8,128)(2,1)S(1)} %get-tuple-element.16), channel_id=1, source_target_pairs={{0,16},{8,24},{16,0},{24,8},{1,17},{9,25},{17,1},{25,9},{2,18},{10... | collective-permute-start | bytes 86024 | tf_op jit(solution)/shard_map/ppermute | solution.py:14
  6.4 8.0 %collective-permute-start.2 = (bf16[28,512]{1,0:T(8,128)(2,1)S(1)}, bf16[28,512]{1,0:T(8,128)(2,1)S(1)}, u32[]{:S(2)}, u32[]{:S(2)}) collective-permute-start(bf16[28,512]{1,0:T(8,128)(2,1)S(1)} %get-tuple-element.16), channel_id=1, source_target_pairs={{0,24},{8,16},{16,8},{24,0},{1,25},{9,17},{17,9},{25,1},{2,26},{10... | collective-permute-start | bytes 86024 | tf_op jit(solution)/shard_map/ppermute | solution.py:14
  9.4 12.8 %all-to-all-start = ((bf16[8,24,1024]{2,1,0:T(8,128)(2,1)}), bf16[8,24,1024]{2,1,0:T(8,128)(2,1)S(1)}, u32[]{:S(2)}, u32[]{:S(2)}) async-start(bf16[8,24,1024]{2,1,0:T(8,128)(2,1)} %bitcast.7), calls=%async_computation | async-start | bytes 786432 | tf_op jit(solution)/shard_map/all_to_all | solution.py:93
  15.1 13.2 %collective-permute-start.3 = (bf16[4,28,512]{2,1,0:T(8,128)(2,1)}, bf16[4,28,512]{2,1,0:T(8,128)(2,1)}, u32[]{:S(2)}, u32[]{:S(2)}) collective-permute-start(bf16[4,28,512]{2,1,0:T(8,128)(2,1)} %pad_maximum_fusion.1), channel_id=1, source_target_pairs={{0,2},{1,3},{2,0},{3,1},{4,6},{5,7},{6,4},{7,5},{8,10},{9,11},{10,... | collective-permute-start | bytes 344072 | tf_op jit(solution)/shard_map/ppermute | solution.py:24
  17.1 11.2 %collective-permute-start.4 = (bf16[4,28,512]{2,1,0:T(8,128)(2,1)}, bf16[4,28,512]{2,1,0:T(8,128)(2,1)}, u32[]{:S(2)}, u32[]{:S(2)}) collective-permute-start(bf16[4,28,512]{2,1,0:T(8,128)(2,1)} %pad_maximum_fusion.1), channel_id=1, source_target_pairs={{0,4},{1,5},{2,6},{3,7},{4,0},{5,1},{6,2},{7,3},{8,12},{9,13},{10,... | collective-permute-start | bytes 344072 | tf_op jit(solution)/shard_map/ppermute | solution.py:24
  18.6 9.7 %collective-permute-start.5 = (bf16[4,28,512]{2,1,0:T(8,128)(2,1)}, bf16[4,28,512]{2,1,0:T(8,128)(2,1)}, u32[]{:S(2)}, u32[]{:S(2)}) collective-permute-start(bf16[4,28,512]{2,1,0:T(8,128)(2,1)} %pad_maximum_fusion.1), channel_id=1, source_target_pairs={{0,6},{1,7},{2,4},{3,5},{4,2},{5,3},{6,0},{7,1},{8,14},{9,15},{10,... | collective-permute-start | bytes 344072 | tf_op jit(solution)/shard_map/ppermute | solution.py:24
  30.3 9.6 %all-to-all-start.1 = ((bf16[8,2,6144]{2,1,0:T(2,128)(2,1)}), bf16[8,2,6144]{2,1,0:T(2,128)(2,1)S(1)}, u32[]{:S(2)}, u32[]{:S(2)}) async-start(bf16[8,2,6144]{2,1,0:T(2,128)(2,1)} %reshape.503), calls=%async_computation.1 | async-start | bytes 393216 | tf_op jit(solution)/shard_map/all_to_all | solution.py:120
  33.7 2.3 %collective-permute-start.6 = (bf16[4,28,512]{2,1,0:T(8,128)(2,1)}, bf16[4,28,512]{2,1,0:T(8,128)(2,1)S(1)}, u32[]{:S(2)}, u32[]{:S(2)}) collective-permute-start(bf16[4,28,512]{2,1,0:T(8,128)(2,1)} %pad_maximum_fusion.1), channel_id=1, source_target_pairs={{0,1},{1,0},{2,3},{3,2},{4,5},{5,4},{6,7},{7,6},{8,9},{9,8},{10,11... | collective-permute-start | bytes 344072 | tf_op jit(solution)/shard_map/ppermute | solution.py:60
  34.1 1.9 %collective-permute-start.7 = (bf16[4,28,512]{2,1,0:T(8,128)(2,1)}, bf16[4,28,512]{2,1,0:T(8,128)(2,1)S(1)}, u32[]{:S(2)}, u32[]{:S(2)}) collective-permute-start(bf16[4,28,512]{2,1,0:T(8,128)(2,1)} %collective-permute-done.3), channel_id=1, source_target_pairs={{0,1},{1,0},{2,3},{3,2},{4,5},{5,4},{6,7},{7,6},{8,9},{9,8},{10,11... | collective-permute-start | bytes 344072 | tf_op jit(solution)/shard_map/ppermute | solution.py:60
  34.3 1.7 %collective-permute-start.8 = (bf16[4,28,512]{2,1,0:T(8,128)(2,1)}, bf16[4,28,512]{2,1,0:T(8,128)(2,1)S(1)}, u32[]{:S(2)}, u32[]{:S(2)}) collective-permute-start(bf16[4,28,512]{2,1,0:T(8,128)(2,1)} %collective-permute-done.4), channel_id=1, source_target_pairs={{0,1},{1,0},{2,3},{3,2},{4,5},{5,4},{6,7},{7,6},{8,9},{9,8},{10,11... | collective-permute-start | bytes 344072 | tf_op jit(solution)/shard_map/ppermute | solution.py:60
  34.6 1.6 %collective-permute-start.9 = (bf16[4,28,512]{2,1,0:T(8,128)(2,1)}, bf16[4,28,512]{2,1,0:T(8,128)(2,1)S(1)}, u32[]{:S(2)}, u32[]{:S(2)}) collective-permute-start(bf16[4,28,512]{2,1,0:T(8,128)(2,1)} %collective-permute-done.5), channel_id=1, source_target_pairs={{0,1},{1,0},{2,3},{3,2},{4,5},{5,4},{6,7},{7,6},{8,9},{9,8},{10,11... | collective-permute-start | bytes 344072 | tf_op jit(solution)/shard_map/ppermute | solution.py:60
  42.3 9.6 %all-to-all-start.2 = ((bf16[8,2,6144]{2,1,0:T(2,128)(2,1)}), bf16[8,2,6144]{2,1,0:T(2,128)(2,1)S(1)}, u32[]{:S(2)}, u32[]{:S(2)}) async-start(bf16[8,2,6144]{2,1,0:T(2,128)(2,1)} %reshape.505), calls=%async_computation.2 | async-start | bytes 393216 | tf_op jit(solution)/shard_map/all_to_all | solution.py:132
  45.8 6.9 %copy-start = (bf16[2,2,64,384]{3,2,1,0:T(8,128)(2,1)S(1)}, bf16[2,2,64,384]{3,2,1,0:T(8,128)(2,1)}, u32[]{:S(2)}) copy-start(bf16[2,2,64,384]{3,2,1,0:T(8,128)(2,1)} %param.13) | copy-start | bytes 589828
